TPU v7x, 512 devices: a whole 4x8x8 slice. The times are simulated.
512 devices in a mesh: req: 64 (over x, z, core), ch: 8 (over y).
Axes of the slice: x: 4, y: 8, z: 8, core: 2. Of those that a mesh axis runs over, the one named last changes fastest.
Arguments:
- tokens: bfloat16 [128, 4096], P('req', 'ch'), may hold values from -80 to 80
- attn_gain: float32 [4096], P('ch'), may hold values from 0.1 to 1.9
- w_query: bfloat16 [4096, 4096], P('ch', 'req'), may hold values from -0.09375 to 0.09375
- w_keyval: bfloat16 [4096, 512], P('ch', 'req'), may hold values from -0.09375 to 0.09375
- cache: bfloat16 [2, 128, 256, 2048], P(None, 'req', 'ch'), may hold values from -70 to 70
- lengths: int32 [128], P('req'), may hold values from 1 to 2047, as said below
- write_pos: int32 [128], P('req'), may hold values from 0 to 2047
- w_out: bfloat16 [4096, 4096], P('ch', 'req'), may hold values from -0.09375 to 0.09375
- mlp_gain: float32 [4096], P('ch'), may hold values from 0.1 to 1.9
- w_gate_up: bfloat16 [4096, 24576], P('ch', 'req'), may hold values from -0.09375 to 0.09375
- w_down: bfloat16 [12288, 4096], P('req', 'ch'), may hold values from -0.0546875 to 0.0546875
Outputs:
- layer_out: bfloat16 [128, 4096], P('req', 'ch')
- kv_new: bfloat16 [128, 512], P('req', 'ch')
Inputs may be any that keep to these rules, and one draw needn't show every extreme that they name: lengths[b] earlier tokens of request b are in the cache; the largest equals 2047 in every draw. The new token of request b goes to slot write_pos[b]; its earlier tokens fill the slots before it, going back cyclically.
All inputs are finite; a program needn't handle non-finite values.
Results may differ from a plain program's by a relative error of at most 0.0064.
Values may be sent and summed in bfloat16 or wider, within the bound.
No kernel may reach another device: no remote copies, remote signals or barrier semaphores. Data moves between devices by JAX's collectives and lax.ppermute only.
A program may use at most 64 MiB of HBM per device.

v0:
```python
import math
import jax
import jax.numpy as jnp
from jax import lax
from jax.sharding import PartitionSpec as P

D = 4096
H = 16
HD = 256
EPSILON = 1e-06


def rms_norm(values, gain):
    wide = values.astype(jnp.float32)
    squares = jnp.sum(wide * wide, axis=1)
    summed = lax.psum(squares, "ch")
    meansq = summed / D
    return (wide * lax.rsqrt(meansq + EPSILON)[:, None] * gain[None, :]).astype(jnp.bfloat16)


def body(
    tokens,
    attn_gain,
    w_query,
    w_keyval,
    cache,
    lengths,
    write_pos,
    w_out,
    mlp_gain,
    w_gate_up,
    w_down,
):
    rows = tokens.shape[0]
    chan = cache.shape[2]
    window = cache.shape[3]
    factor = 1.0 / math.sqrt(HD)
    normed = rms_norm(tokens, attn_gain)
    joined = jnp.concatenate([w_query, w_keyval], axis=1)
    head_parts = jnp.dot(
        lax.all_gather(normed, "req", axis=0, tiled=True),
        joined,
        preferred_element_type=jnp.float32,
    )
    query_cols = w_query.shape[1]
    query_part, keyval_part = (
        lax.all_to_all(head_parts[:, :query_cols], "req", split_axis=0, concat_axis=1, tiled=True),
        lax.all_to_all(head_parts[:, query_cols:], "req", split_axis=0, concat_axis=1, tiled=True),
    )
    query_sum, keyval_sum = (
        lax.psum_scatter(query_part, "ch", scatter_dimension=1, tiled=True),
        lax.psum_scatter(keyval_part, "ch", scatter_dimension=1, tiled=True),
    )
    queries = query_sum.astype(jnp.bfloat16).reshape(rows, H, chan)
    keyval_new = keyval_sum.astype(jnp.bfloat16)
    key_new = keyval_new[:, :chan]
    value_new = keyval_new[:, chan:]
    keys = cache[0]
    values_cache = cache[1]
    own_part = jnp.sum(
        queries.astype(jnp.float32) * key_new.astype(jnp.float32)[:, None, :], axis=-1
    )
    score_part = jnp.einsum("bhe,bew->bhw", queries, keys, preferred_element_type=jnp.float32)
    summed, own_sum = lax.psum((score_part, own_part), "ch")
    slot_index = jnp.arange(window, dtype=jnp.int32)
    offset = (write_pos[:, None] - 1 - slot_index[None, :]) % window
    usable = offset < lengths[:, None]
    scores = jnp.where(usable[:, None, :], summed * factor, -jnp.inf)
    own_score = own_sum * factor
    top = jnp.maximum(jnp.max(scores, axis=-1), own_score)
    weights = jnp.exp(scores - top[..., None])
    own_weight = jnp.exp(own_score - top)
    total = jnp.sum(weights, axis=-1) + own_weight
    weights_low = weights.astype(jnp.bfloat16)
    numer = jnp.einsum(
        "bhw,bew->bhe", weights_low, values_cache, preferred_element_type=jnp.float32
    )
    numer = (
        numer
        + own_weight.astype(jnp.bfloat16).astype(jnp.float32)[..., None]
        * value_new.astype(jnp.float32)[:, None, :]
    )
    attn_local = (numer / total[..., None]).astype(jnp.bfloat16).reshape(rows, H * chan)
    out_parts = jnp.dot(
        lax.all_gather(attn_local, "req", axis=0, tiled=True),
        w_out,
        preferred_element_type=jnp.float32,
    )
    out_part = lax.all_to_all(out_parts, "req", split_axis=0, concat_axis=1, tiled=True)
    out_sum = lax.psum_scatter(out_part, "ch", scatter_dimension=1, tiled=True)
    first = (tokens.astype(jnp.float32) + out_sum).astype(jnp.bfloat16)
    normed_two = rms_norm(first, mlp_gain)
    hidden_cols = w_gate_up.shape[1] // 2
    ffn_parts = jnp.dot(
        lax.all_gather(normed_two, "req", axis=0, tiled=True),
        w_gate_up,
        preferred_element_type=jnp.float32,
    )
    ffn_total = lax.psum(ffn_parts, "ch")
    hidden = (
        jax.nn.gelu(ffn_total[:, :hidden_cols], approximate=True) * ffn_total[:, hidden_cols:]
    ).astype(jnp.bfloat16)
    down_sum = lax.psum_scatter(
        jnp.dot(hidden, w_down, preferred_element_type=jnp.float32),
        "req",
        scatter_dimension=0,
        tiled=True,
    )
    layer_out = (first.astype(jnp.float32) + down_sum).astype(jnp.bfloat16)
    return (layer_out, keyval_new)


def solution(mesh):
    placed = (
        P("req", "ch"),
        P("ch"),
        P("ch", "req"),
        P("ch", "req"),
        P(None, "req", "ch", None),
        P("req"),
        P("req"),
        P("ch", "req"),
        P("ch"),
        P("ch", "req"),
        P("req", "ch"),
    )
    return jax.shard_map(
        body,
        mesh=mesh,
        in_specs=placed,
        out_specs=(P("req", "ch"), P("req", "ch")),
        check_vma=False,
    )
```

profile of v0, /device:TPU:1, one launch (start us, length us, event | category | flops | bytes accessed | tf_op | source)
XLA Modules:
  0.0 728.1 jit_solution(11447148937282177522)
XLA Ops:
  7.2 0.8 fusion.36
  8.0 14.7 %psum.35 = f32[2]{0:T(128)S(1)} all-reduce(f32[2]{0:T(128)S(1)} %fusion.36), channel_id=1, replica_groups=mesh['req'=64,'ch'=8] {'ch'}, use_global_device_ids=true, to_apply=%region_1.0 | all-reduce | flops 2 | bytes 16 | tf_op jit(solution)/shard_map/psum | solution.py:16
  23.5 60.2 %all-gather = bf16[64,2,512]{2,1,0:T(2,128)(2,1)S(1)} all-gather(bf16[1,2,512]{2,1,0:T(2,128)(2,1)S(1)} %fusion.45), channel_id=1, replica_groups=mesh['req'=64,'ch'=8] {'req'}, dimensions={0}, use_global_device_ids=true | all-gather | bytes 133120 | tf_op jit(solution)/shard_map/all_gather | solution.py:41
  83.7 1.0 fusion.24
  85.5 5.6 all-to-all-start.1
  91.9 8.9 %all-to-all-done.1 = f32[64,2,8]{2,1,0:T(2,128)S(1)} async-done(((f32[64,2,8]{2,1,0:T(2,128)}), f32[64,2,8]{2,1,0:T(2,128)S(1)}, u32[]{:S(2)}, u32[]{:S(2)}) %all-to-all-start.1) | async-done | bytes 4128 | tf_op jit(solution)/shard_map/all_to_all | solution.py:48
  100.8 4.4 all-to-all-start
  105.2 1.2 copy.40
  107.2 7.5 %all-to-all-done = f32[64,1,128]{2,1,0:T(1,128)S(1)} async-done(((f32[64,1,128]{2,1,0:T(1,128)}), f32[64,1,128]{2,1,0:T(1,128)S(1)}, u32[]{:S(2)}, u32[]{:S(2)}) %all-to-all-start) | async-done | bytes 32800 | tf_op jit(solution)/shard_map/all_to_all | solution.py:47
  116.0 2.0 copy.39
  118.2 23.1 %reduce-scatter.12.cloned.1.call-done = f32[64,2]{1,0:T(8,128)} async-done(((f32[512,2]{1,0:T(8,128)}), f32[64,2]{1,0:T(8,128)}) %reduce-scatter.12.cloned.1.call-update) | async-done | bytes 528
  142.2 47.1 %reduce-scatter.10.cloned.1.call-done = f32[512,2]{1,0:T(8,128)} async-done(((f32[4096,2]{1,0:T(8,128)}), f32[512,2]{1,0:T(8,128)}) %reduce-scatter.10.cloned.1.call-update) | async-done | bytes 4112
  189.3 1.1 copy.34
  190.5 0.9 fusion.3
  191.6 11.9 %psum.37 = f32[2,16]{1,0:T(2,128)S(1)} all-reduce(f32[2,16]{1,0:T(2,128)S(1)} %multiply_reduce_fusion), channel_id=1, replica_groups=mesh['req'=64,'ch'=8] {'ch'}, use_global_device_ids=true, to_apply=%region_7.8 | all-reduce | flops 32 | bytes 256 | tf_op jit(solution)/shard_map/psum | solution.py:64
  203.5 64.4 %all-reduce.5.cloned.1.call-done = f32[2,16,2048]{2,1,0:T(8,128)} async-done(((f32[2,16,2048]{2,1,0:T(8,128)}), f32[2,16,2048]{2,1,0:T(8,128)}) %all-reduce.5.cloned.1.call-update) | async-done | bytes 262160 | tf_op jit(solution)/shard_map/psum | solution.py:64
  267.9 1.1 fusion.7
  269.0 1.2 fusion.8
  270.1 1.2 fusion.1
  271.4 57.0 %all-gather.1 = bf16[64,2,512]{2,1,0:T(2,128)(2,1)S(1)} all-gather(bf16[1,2,512]{2,1,0:T(2,128)(2,1)S(1)} %reshape.73), channel_id=1, replica_groups=mesh['req'=64,'ch'=8] {'req'}, dimensions={0}, use_global_device_ids=true | all-gather | bytes 133120 | tf_op jit(solution)/shard_map/all_gather | solution.py:85
  328.8 16.1 %all_to_all.57 = f32[64,1,128]{2,1,0:T(1,128)S(1)} all-to-all(f32[64,1,128]{2,1,0:T(1,128)S(1)} %reshape.87), channel_id=1, replica_groups=mesh['req'=64,'ch'=8] {'req'}, dimensions={0} | all-to-all | bytes 65536 | tf_op jit(solution)/shard_map/all_to_all | solution.py:89
  345.8 2.0 copy.41
  347.9 32.4 %reduce-scatter.14.cloned.1.call-done = f32[512,2]{1,0:T(8,128)} async-done(((f32[4096,2]{1,0:T(8,128)}), f32[512,2]{1,0:T(8,128)}) %reduce-scatter.14.cloned.1.call-update) | async-done | bytes 4112
  380.3 1.1 copy.38
  381.5 12.0 %psum.38 = f32[2]{0:T(128)S(1)} all-reduce(f32[2]{0:T(128)S(1)} %get-tuple-element.2), channel_id=1, replica_groups=mesh['req'=64,'ch'=8] {'ch'}, use_global_device_ids=true, to_apply=%region_11.12 | all-reduce | flops 2 | bytes 16 | tf_op jit(solution)/shard_map/psum | solution.py:16
  393.6 59.6 %all-gather.2 = bf16[64,2,512]{2,1,0:T(2,128)(2,1)S(1)} all-gather(bf16[1,2,512]{2,1,0:T(2,128)(2,1)S(1)} %fusion.44), channel_id=1, replica_groups=mesh['req'=64,'ch'=8] {'req'}, dimensions={0}, use_global_device_ids=true | all-gather | bytes 133120 | tf_op jit(solution)/shard_map/all_gather | solution.py:95
  453.2 0.9 fusion.56
  454.2 69.2 %all-reduce.7.cloned.1.call-done = f32[128,384]{1,0:T(8,128)} async-done(((f32[128,384]{1,0:T(8,128)}), f32[128,384]{1,0:T(8,128)}) %all-reduce.7.cloned.1.call-update) | async-done | bytes 196624 | tf_op jit(solution)/shard_map/psum | solution.py:99
  523.4 1.9 fusion.28
  525.3 1.3 dynamic-slice
  527.3 192.7 %all-reduce.9.cloned.1.call-done = f32[128,512]{1,0:T(8,128)} async-done(((f32[128,512]{1,0:T(8,128)}), f32[128,512]{1,0:T(8,128)}) %all-reduce.9.cloned.1.call-update) | async-done | bytes 262160
  720.0 1.3 fusion.43
  (57 shorter events, 7.5 us)
Async XLA Ops:
  7.2 446.1 %copy-start = (bf16[512,384]{1,0:T(8,128)(2,1)S(1)}, bf16[512,384]{1,0:T(8,128)(2,1)}, u32[]{:S(2)}) copy-start(bf16[512,384]{1,0:T(8,128)(2,1)} %param.20) | copy-start | bytes 1179652
  85.5 15.3 %all-to-all-start.1 = ((f32[64,2,8]{2,1,0:T(2,128)}), f32[64,2,8]{2,1,0:T(2,128)S(1)}, u32[]{:S(2)}, u32[]{:S(2)}) async-start(f32[64,2,8]{2,1,0:T(2,128)} %bitcast.4), calls=%async_computation.1 | async-start | bytes 131072 | tf_op jit(solution)/shard_map/all_to_all | solution.py:48
  100.8 13.8 %all-to-all-start = ((f32[64,1,128]{2,1,0:T(1,128)}), f32[64,1,128]{2,1,0:T(1,128)S(1)}, u32[]{:S(2)}, u32[]{:S(2)}) async-start(f32[64,1,128]{2,1,0:T(1,128)} %reshape.85), calls=%async_computation | async-start | bytes 65536 | tf_op jit(solution)/shard_map/all_to_all | solution.py:47
  105.2 36.1 %reduce-scatter.12.cloned.1.call-start = ((), (), s32[]{:S(2)}) async-start(), calls=%async_computation.9 | async-start | bytes 294912
  106.4 82.9 %reduce-scatter.10.cloned.1.call-start = ((), (), s32[]{:S(2)}) async-start(), calls=%async_computation.8 | async-start | bytes 2359296
  116.0 2.2 copy-start.7
  116.0 74.5 %copy-start.2 = (bf16[2,2,32,2048]{3,2,1,0:T(8,128)(2,1)S(1)}, bf16[2,2,32,2048]{3,2,1,0:T(8,128)(2,1)}, u32[]{:S(2)}) copy-start(bf16[2,2,32,2048]{3,2,1,0:T(8,128)(2,1)} %param.15) | copy-start | bytes 1572868
  118.0 210.5 %copy-start.3 = (bf16[512,64]{0,1:T(8,128)(2,1)S(1)}, bf16[512,64]{0,1:T(8,128)(2,1)}, u32[]{:S(2)}) copy-start(bf16[512,64]{0,1:T(8,128)(2,1)} %param.18) | copy-start | bytes 196612
  118.1 149.8 %all-reduce.5.cloned.1.call-start = ((), (), s32[]{:S(2)}) async-start(), calls=%async_computation.6 | async-start | bytes 524288 | tf_op jit(solution)/shard_map/psum | solution.py:64
  142.2 205.6 %copy-start.5 = (bf16[2,64]{1,0:T(2,128)(2,1)}, bf16[2,64]{1,0:T(2,128)(2,1)S(1)}, u32[]{:S(2)}) copy-start(bf16[2,64]{1,0:T(2,128)(2,1)S(1)} %copy.36) | copy-start | bytes 772
  191.4 188.9 %reduce-scatter.14.cloned.1.call-start = ((), (), s32[]{:S(2)}) async-start(), calls=%async_computation.10 | async-start | bytes 2359296
  345.7 35.6 %copy-start.4 = (bf16[2,512]{1,0:T(2,128)(2,1)S(1)}, bf16[2,512]{1,0:T(2,128)(2,1)}, u32[]{:S(2)}) copy-start(bf16[2,512]{1,0:T(2,128)(2,1)} %param.11) | copy-start | bytes 6148
  345.8 47.8 %copy-start.6 = (f32[512]{0:T(512)S(1)}, f32[512]{0:T(512)}, u32[]{:S(2)}) copy-start(f32[512]{0:T(512)} %param.19) | copy-start | bytes 6148
  347.8 175.6 %copy-start.1 = (bf16[192,512]{1,0:T(8,128)(2,1)S(1)}, bf16[192,512]{1,0:T(8,128)(2,1)}, u32[]{:S(2)}) copy-start(bf16[192,512]{1,0:T(8,128)(2,1)} %param.21) | copy-start | bytes 589828
  347.8 175.6 %all-reduce.7.cloned.1.call-start = ((), (), s32[]{:S(2)}) async-start(), calls=%async_computation.7 | async-start | bytes 393216 | tf_op jit(solution)/shard_map/psum | solution.py:99
  454.2 265.8 %all-reduce.9.cloned.1.call-start = ((), (), s32[]{:S(2)}) async-start(), calls=%async_computation.11 | async-start | bytes 524288
Sparse Core Ops, SparseCore 0:
  108.8 32.4 reduce-scatter.11
  144.2 45.0 reduce-scatter.9
  191.6 76.2 all-reduce.4
  348.0 32.2 reduce-scatter.13
  454.3 69.0 all-reduce.6
  526.7 193.2 all-reduce.8
where the time goes:
time: 729 us; the launch traced here: 728 us
  waiting for transfers between devices  446 us (61%)
  blocking collectives  231 us (32%)
  between operations  15 us (2%)
  local copies, waits for them, and re-layouts  12.2 us (2%)
  starting transfers between devices  10.2 us (1%)
  other arithmetic  7.74 us (1%)
    unnamed x10, waiting for transfers between devices  295 us
    psum x1, waiting for transfers between devices, body(): ffn_total = lax.psum(ffn_parts, 'ch')  69.2 us
    psum x1, waiting for transfers between devices, body(): summed, own_sum = lax.psum((score_part, own_part), 'ch')  64.4 us
    all_gather x1, blocking collectives, body(): lax.all_gather(normed, 'req', axis=0, tiled=True)  60.2 us
    all_gather x1, blocking collectives, body(): lax.all_gather(normed_two, 'req', axis=0, tiled=True)  59.6 us
    all_gather x1, blocking collectives, body(): lax.all_gather(attn_local, 'req', axis=0, tiled=True)  57 us
    psum x2, blocking collectives, rms_norm(): summed = lax.psum(squares, 'ch')  26.7 us
    all_to_all x1, blocking collectives, body(): lax.all_to_all(out_parts, 'req', split_axis=0, concat_axis=1, tiled=True)  16.1 us
  transfers between devices with their start and end apart: 8, of which 8 were waited for; matrix products, arithmetic and copies ran while one was open for 1% of the time, Pallas kernels for 0%

commit v1 on v0

--- a/solution.py
+++ b/solution.py
@@ -38,7 +38,9 @@
     normed = rms_norm(tokens, attn_gain)
     joined = jnp.concatenate([w_query, w_keyval], axis=1)
     head_parts = jnp.dot(
-        lax.all_gather(normed, "req", axis=0, tiled=True),
+        jnp.concatenate(
+            lax.all_to_all(jnp.stack([normed] * lax.axis_size("req")), "req", 0, 0), axis=0
+        ),
         joined,
         preferred_element_type=jnp.float32,
     )

time: 729 us -> 696 us (0.955)
  blocking collectives: 231 us -> 199 us
    all_gather x1 -> x0, blocking collectives: 60.2 us -> none  [body(): lax.all_gather(normed, 'req', axis=0, tiled=True)]
    all_to_all x0 -> x1, blocking collectives: none -> 27.9 us  [body(): lax.all_to_all(jnp.stack([normed] * lax.axis_size('req')), 'req', 0, 0)]
where the time goes in v1:
time: 696 us; the launch traced here: 695 us
  waiting for transfers between devices  446 us (64%)
  blocking collectives  199 us (29%)
  between operations  15 us (2%)
  local copies, waits for them, and re-layouts  12.3 us (2%)
  starting transfers between devices  9.49 us (1%)
  other arithmetic  7.74 us (1%)
    unnamed x10, waiting for transfers between devices  296 us
    psum x1, waiting for transfers between devices, body(): ffn_total = lax.psum(ffn_parts, 'ch')  69.1 us
    psum x1, waiting for transfers between devices, body(): summed, own_sum = lax.psum((score_part, own_part), 'ch')  64.5 us
    all_gather x1, blocking collectives, body(): lax.all_gather(normed_two, 'req', axis=0, tiled=True)  59.8 us
    all_gather x1, blocking collectives, body(): lax.all_gather(attn_local, 'req', axis=0, tiled=True)  57 us
    all_to_all x1, blocking collectives, body(): lax.all_to_all(jnp.stack([normed] * lax.axis_size('req')), 'req', 0, 0)  27.9 us
    psum x2, blocking collectives, rms_norm(): summed = lax.psum(squares, 'ch')  26.5 us
    all_to_all x1, blocking collectives, body(): lax.all_to_all(out_parts, 'req', split_axis=0, concat_axis=1, tiled=True)  16.1 us
  transfers between devices with their start and end apart: 8, of which 8 were waited for; matrix products, arithmetic and copies ran while one was open for 1% of the time, Pallas kernels for 0%

profile of v1, /device:TPU:1, one launch (start us, length us, event | category | flops | bytes accessed | tf_op | source)
XLA Modules:
  0.0 695.2 jit_solution(9891826642196067593)
XLA Ops:
  7.2 0.8 fusion.36
  8.0 14.7 %psum.35 = f32[2]{0:T(128)S(1)} all-reduce(f32[2]{0:T(128)S(1)} %fusion.36), channel_id=1, replica_groups=mesh['req'=64,'ch'=8] {'ch'}, use_global_device_ids=true, to_apply=%region_1.0 | all-reduce | flops 2 | bytes 16 | tf_op jit(solution)/shard_map/psum | solution.py:16
  23.6 27.9 %all_to_all.62 = bf16[64,2,512]{2,1,0:T(2,128)(2,1)S(1)} all-to-all(bf16[64,2,512]{2,1,0:T(2,128)(2,1)S(1)} %stack.2), channel_id=1, replica_groups=mesh['req'=64,'ch'=8] {'req'}, dimensions={0} | all-to-all | bytes 262144 | tf_op jit(solution)/shard_map/all_to_all | solution.py:42
  51.5 1.0 fusion.24
  53.3 4.9 all-to-all-start.2
  59.0 8.9 %all-to-all-done.2 = f32[64,2,8]{2,1,0:T(2,128)S(1)} async-done(((f32[64,2,8]{2,1,0:T(2,128)}), f32[64,2,8]{2,1,0:T(2,128)S(1)}, u32[]{:S(2)}, u32[]{:S(2)}) %all-to-all-start.2) | async-done | bytes 4128 | tf_op jit(solution)/shard_map/all_to_all | solution.py:50
  68.0 4.4 all-to-all-start.1
  72.4 1.2 copy.40
  74.3 7.5 %all-to-all-done.1 = f32[64,1,128]{2,1,0:T(1,128)S(1)} async-done(((f32[64,1,128]{2,1,0:T(1,128)}), f32[64,1,128]{2,1,0:T(1,128)S(1)}, u32[]{:S(2)}, u32[]{:S(2)}) %all-to-all-start.1) | async-done | bytes 32800 | tf_op jit(solution)/shard_map/all_to_all | solution.py:49
  83.1 2.0 copy.39
  85.4 23.1 %reduce-scatter.12.cloned.1.call-done = f32[64,2]{1,0:T(8,128)} async-done(((f32[512,2]{1,0:T(8,128)}), f32[64,2]{1,0:T(8,128)}) %reduce-scatter.12.cloned.1.call-update) | async-done | bytes 528
  109.3 47.2 %reduce-scatter.10.cloned.1.call-done = f32[512,2]{1,0:T(8,128)} async-done(((f32[4096,2]{1,0:T(8,128)}), f32[512,2]{1,0:T(8,128)}) %reduce-scatter.10.cloned.1.call-update) | async-done | bytes 4112
  156.5 1.1 copy.34
  157.7 0.9 fusion.3
  158.8 11.8 %psum.37 = f32[2,16]{1,0:T(2,128)S(1)} all-reduce(f32[2,16]{1,0:T(2,128)S(1)} %multiply_reduce_fusion), channel_id=1, replica_groups=mesh['req'=64,'ch'=8] {'ch'}, use_global_device_ids=true, to_apply=%region_7.8 | all-reduce | flops 32 | bytes 256 | tf_op jit(solution)/shard_map/psum | solution.py:66
  170.6 64.5 %all-reduce.5.cloned.1.call-done = f32[2,16,2048]{2,1,0:T(8,128)} async-done(((f32[2,16,2048]{2,1,0:T(8,128)}), f32[2,16,2048]{2,1,0:T(8,128)}) %all-reduce.5.cloned.1.call-update) | async-done | bytes 262160 | tf_op jit(solution)/shard_map/psum | solution.py:66
  235.0 1.1 fusion.7
  236.1 1.2 fusion.8
  237.3 1.2 fusion.1
  238.6 57.0 %all-gather = bf16[64,2,512]{2,1,0:T(2,128)(2,1)S(1)} all-gather(bf16[1,2,512]{2,1,0:T(2,128)(2,1)S(1)} %reshape.77), channel_id=1, replica_groups=mesh['req'=64,'ch'=8] {'req'}, dimensions={0}, use_global_device_ids=true | all-gather | bytes 133120 | tf_op jit(solution)/shard_map/all_gather | solution.py:87
  295.9 16.1 %all_to_all.63 = f32[64,1,128]{2,1,0:T(1,128)S(1)} all-to-all(f32[64,1,128]{2,1,0:T(1,128)S(1)} %reshape.91), channel_id=1, replica_groups=mesh['req'=64,'ch'=8] {'req'}, dimensions={0} | all-to-all | bytes 65536 | tf_op jit(solution)/shard_map/all_to_all | solution.py:91
  312.9 2.0 copy.41
  315.0 32.4 %reduce-scatter.14.cloned.1.call-done = f32[512,2]{1,0:T(8,128)} async-done(((f32[4096,2]{1,0:T(8,128)}), f32[512,2]{1,0:T(8,128)}) %reduce-scatter.14.cloned.1.call-update) | async-done | bytes 4112
  347.4 1.1 copy.38
  348.6 11.8 %psum.38 = f32[2]{0:T(128)S(1)} all-reduce(f32[2]{0:T(128)S(1)} %get-tuple-element.2), channel_id=1, replica_groups=mesh['req'=64,'ch'=8] {'ch'}, use_global_device_ids=true, to_apply=%region_11.12 | all-reduce | flops 2 | bytes 16 | tf_op jit(solution)/shard_map/psum | solution.py:16
  360.5 59.8 %all-gather.1 = bf16[64,2,512]{2,1,0:T(2,128)(2,1)S(1)} all-gather(bf16[1,2,512]{2,1,0:T(2,128)(2,1)S(1)} %fusion.44), channel_id=1, replica_groups=mesh['req'=64,'ch'=8] {'req'}, dimensions={0}, use_global_device_ids=true | all-gather | bytes 133120 | tf_op jit(solution)/shard_map/all_gather | solution.py:97
  420.4 0.9 fusion.55
  421.4 69.1 %all-reduce.7.cloned.1.call-done = f32[128,384]{1,0:T(8,128)} async-done(((f32[128,384]{1,0:T(8,128)}), f32[128,384]{1,0:T(8,128)}) %all-reduce.7.cloned.1.call-update) | async-done | bytes 196624 | tf_op jit(solution)/shard_map/psum | solution.py:101
  490.5 1.9 fusion.28
  492.4 1.3 dynamic-slice
  494.3 192.7 %all-reduce.9.cloned.1.call-done = f32[128,512]{1,0:T(8,128)} async-done(((f32[128,512]{1,0:T(8,128)}), f32[128,512]{1,0:T(8,128)}) %all-reduce.9.cloned.1.call-update) | async-done | bytes 262160
  687.1 1.3 fusion.43
  (58 shorter events, 7.5 us)
Async XLA Ops:
  7.2 413.2 %copy-start = (bf16[512,384]{1,0:T(8,128)(2,1)S(1)}, bf16[512,384]{1,0:T(8,128)(2,1)}, u32[]{:S(2)}) copy-start(bf16[512,384]{1,0:T(8,128)(2,1)} %param.20) | copy-start | bytes 1179652
  53.3 14.7 %all-to-all-start.2 = ((f32[64,2,8]{2,1,0:T(2,128)}), f32[64,2,8]{2,1,0:T(2,128)S(1)}, u32[]{:S(2)}, u32[]{:S(2)}) async-start(f32[64,2,8]{2,1,0:T(2,128)} %bitcast.3), calls=%async_computation.2 | async-start | bytes 131072 | tf_op jit(solution)/shard_map/all_to_all | solution.py:50
  68.0 13.8 %all-to-all-start.1 = ((f32[64,1,128]{2,1,0:T(1,128)}), f32[64,1,128]{2,1,0:T(1,128)S(1)}, u32[]{:S(2)}, u32[]{:S(2)}) async-start(f32[64,1,128]{2,1,0:T(1,128)} %reshape.89), calls=%async_computation.1 | async-start | bytes 65536 | tf_op jit(solution)/shard_map/all_to_all | solution.py:49
  72.3 36.1 %reduce-scatter.12.cloned.1.call-start = ((), (), s32[]{:S(2)}) async-start(), calls=%async_computation.10 | async-start | bytes 294912
  73.6 83.0 %reduce-scatter.10.cloned.1.call-start = ((), (), s32[]{:S(2)}) async-start(), calls=%async_computation.9 | async-start | bytes 2359296
  83.1 2.1 copy-start.7
  83.1 74.6 %copy-start.2 = (bf16[2,2,32,2048]{3,2,1,0:T(8,128)(2,1)S(1)}, bf16[2,2,32,2048]{3,2,1,0:T(8,128)(2,1)}, u32[]{:S(2)}) copy-start(bf16[2,2,32,2048]{3,2,1,0:T(8,128)(2,1)} %param.15) | copy-start | bytes 1572868
  85.2 210.5 %copy-start.3 = (bf16[512,64]{0,1:T(8,128)(2,1)S(1)}, bf16[512,64]{0,1:T(8,128)(2,1)}, u32[]{:S(2)}) copy-start(bf16[512,64]{0,1:T(8,128)(2,1)} %param.18) | copy-start | bytes 196612
  85.2 149.8 %all-reduce.5.cloned.1.call-start = ((), (), s32[]{:S(2)}) async-start(), calls=%async_computation.7 | async-start | bytes 524288 | tf_op jit(solution)/shard_map/psum | solution.py:66
  109.3 205.6 %copy-start.5 = (bf16[2,64]{1,0:T(2,128)(2,1)}, bf16[2,64]{1,0:T(2,128)(2,1)S(1)}, u32[]{:S(2)}) copy-start(bf16[2,64]{1,0:T(2,128)(2,1)S(1)} %copy.36) | copy-start | bytes 772
  158.6 188.9 %reduce-scatter.14.cloned.1.call-start = ((), (), s32[]{:S(2)}) async-start(), calls=%async_computation.11 | async-start | bytes 2359296
  312.9 35.6 %copy-start.4 = (bf16[2,512]{1,0:T(2,128)(2,1)S(1)}, bf16[2,512]{1,0:T(2,128)(2,1)}, u32[]{:S(2)}) copy-start(bf16[2,512]{1,0:T(2,128)(2,1)} %param.11) | copy-start | bytes 6148
  312.9 47.6 %copy-start.6 = (f32[512]{0:T(512)S(1)}, f32[512]{0:T(512)}, u32[]{:S(2)}) copy-start(f32[512]{0:T(512)} %param.19) | copy-start | bytes 6148
  314.9 175.5 %copy-start.1 = (bf16[192,512]{1,0:T(8,128)(2,1)S(1)}, bf16[192,512]{1,0:T(8,128)(2,1)}, u32[]{:S(2)}) copy-start(bf16[192,512]{1,0:T(8,128)(2,1)} %param.21) | copy-start | bytes 589828
  315.0 175.5 %all-reduce.7.cloned.1.call-start = ((), (), s32[]{:S(2)}) async-start(), calls=%async_computation.8 | async-start | bytes 393216 | tf_op jit(solution)/shard_map/psum | solution.py:101
  421.3 265.7 %all-reduce.9.cloned.1.call-start = ((), (), s32[]{:S(2)}) async-start(), calls=%async_computation.12 | async-start | bytes 524288
Sparse Core Ops, SparseCore 0:
  75.9 32.4 reduce-scatter.11
  111.3 45.1 reduce-scatter.9
  158.8 76.1 all-reduce.4
  315.1 32.2 reduce-scatter.13
  421.4 68.9 all-reduce.6
  493.8 193.2 all-reduce.8
